TPU v7x, 512 devices: a whole 4x8x8 slice. The times are simulated.
512 devices in a mesh: node: 32 (over x, y), tile: 16 (over z, core).
Axes of the slice: x: 4, y: 8, z: 8, core: 2. Of those that a mesh axis runs over, the one named last changes fastest.
Arguments:
- states: bfloat16 [196608, 128], P(('node', 'tile')), may hold values from -6 to 6
- adjacency: bfloat16 [65536, 128, 128], P(('node', 'tile')), may hold values from -0.5 to 0.5
- tile_node: int32 [512, 128], P(('node', 'tile')), may hold values from 0 to 31
- tile_block: int32 [512, 128], P(('node', 'tile')), may hold values from 0 to 1, as said below
- tile_rel: int32 [512, 128], P(('node', 'tile')), may hold values from 0 to 534
- tile_dst: int32 [512, 128], P(('node', 'tile')), may hold values from 0 to 47
- send_blocks: int32 [512, 32, 2], P(('node', 'tile')), may hold values from 0 to 2
- send_count: int32 [512, 32], P(('node', 'tile')), may hold values from 1 to 2, as said below
- active: int32 [2, 1536], P(None, ('node', 'tile')), may hold values 0 or 1
- relations: bfloat16 [535, 128], replicated, may hold values from -6 to 6
- mix_weight: bfloat16 [2, 64, 64], replicated, may hold values from -0.75 to 0.75
- norm_gain: float32 [2, 64], replicated, may hold values from 0.5 to 1.5
Outputs:
- new_states: bfloat16 [196608, 128], P(('node', 'tile'))
Inputs may be any that keep to these rules, and one draw needn't show every extreme that they name: On each device, the first send_count entries of each list are distinct; every device has one list with all 2 slots used. For tile t of device n * 16 + j, tile_block[d, t] is less than send_count[a * 16 + j, n], where a = tile_node[d, t].
All inputs are finite; a program needn't handle non-finite values. No bound on the sum of `active` on one device may be relied on, other than what follows from the above.
Results may differ from a plain program's by a relative error of at most 0.02.
Values may be sent and summed in bfloat16 or wider, within the bound.
No kernel may reach another device: no remote copies, remote signals or barrier semaphores. Data moves between devices by JAX's collectives and lax.ppermute only.
A program may use at most 64 MiB of HBM per device.

v0:
```python
import jax
import jax.numpy as jnp
import numpy as np
from jax import lax
from jax.sharding import Mesh
from jax.sharding import PartitionSpec as P

NODE_AXES = ("x", "y")
TILE_AXES = ("z", "core")
ALL_AXES = NODE_AXES + TILE_AXES


def body(
    states,
    adjacency,
    tile_node,
    tile_block,
    tile_rel,
    tile_dst,
    send_blocks,
    send_count,
    active,
    relations,
    mix_weight,
    norm_gain,
):
    size_block = adjacency.shape[1]
    width = states.shape[1]
    own_blocks = states.shape[0] // size_block
    n_z = lax.axis_size("z")
    n_core = lax.axis_size("core")
    group_blocks = own_blocks * n_z * n_core
    tiles_here = adjacency.shape[0]
    depth = mix_weight.shape[1]
    query_count = width // depth
    me_node = lax.axis_index("x") * lax.axis_size("y") + lax.axis_index("y")
    lists_all = lax.all_gather(send_blocks[0], NODE_AXES, axis=0, tiled=False)
    counts_all = lax.all_gather(send_count[0], NODE_AXES, axis=0, tiled=False)
    lists_mine = lax.dynamic_index_in_dim(lists_all, me_node, axis=1, keepdims=False)
    counts_mine = lax.dynamic_index_in_dim(counts_all, me_node, axis=1, keepdims=False)
    sender = tile_node[0]
    slot = tile_block[0]
    local_block = jnp.clip(lists_mine[sender, slot], 0, own_blocks - 1)
    valid = (slot < counts_mine[sender]).astype(jnp.float32)
    source_index = sender * own_blocks + local_block
    rel_onehot = (
        tile_rel[0][:, None] == jnp.arange(relations.shape[0], dtype=jnp.int32)[None, :]
    ).astype(jnp.bfloat16)
    rel_rows = jnp.dot(rel_onehot, relations, preferred_element_type=jnp.float32)
    rel_rows = rel_rows * valid[:, None]
    dst_onehot = (
        jnp.arange(group_blocks, dtype=jnp.int32)[:, None] == tile_dst[0][None, :]
    ).astype(jnp.bfloat16)
    for layer in range(mix_weight.shape[0]):
        blocks = states.reshape(own_blocks, size_block, width) * active[layer][
            :, None, None
        ].astype(jnp.bfloat16)
        gathered = lax.all_gather(blocks, NODE_AXES, axis=0, tiled=True)
        source_rows = jnp.take(gathered, source_index, axis=0)
        modulated = (source_rows * rel_rows[:, None, :]).astype(jnp.bfloat16)
        products = jnp.einsum(
            "tij,tjf->tif", adjacency, modulated, preferred_element_type=jnp.float32
        )
        flat_products = products.reshape(tiles_here, -1)
        high_part = flat_products.astype(jnp.bfloat16)
        low_part = (flat_products - high_part.astype(jnp.float32)).astype(jnp.bfloat16)
        partial_sum = jnp.dot(dst_onehot, high_part, preferred_element_type=jnp.float32) + jnp.dot(
            dst_onehot, low_part, preferred_element_type=jnp.float32
        )
        partial_sum = partial_sum.astype(jnp.bfloat16).reshape(
            n_z, n_core, own_blocks * size_block, width
        )
        by_core = jnp.swapaxes(partial_sum, 0, 1).reshape(-1, width)
        half = lax.psum_scatter(by_core, "core", scatter_dimension=0, tiled=True)
        summed = lax.psum_scatter(half, "z", scatter_dimension=0, tiled=True)
        mixer = jnp.kron(jnp.eye(query_count, dtype=jnp.bfloat16), mix_weight[layer])
        mixed = jnp.dot(summed, mixer, preferred_element_type=jnp.float32).reshape(
            -1, query_count, depth
        )
        center = jnp.mean(mixed, axis=-1, keepdims=True)
        spread = jnp.mean(jnp.square(mixed - center), axis=-1, keepdims=True)
        normed = (mixed - center) * lax.rsqrt(spread + 1e-05) * norm_gain[layer]
        states = (states.astype(jnp.float32) + jax.nn.relu(normed).reshape(-1, width)).astype(
            jnp.bfloat16
        )
    return states


def solution(mesh):
    n_node, n_tile = mesh.devices.shape
    n_x = 4 if n_node % 4 == 0 else 1
    n_y = n_node // n_x
    fine = Mesh(np.asarray(mesh.devices).reshape(n_x, n_y, n_tile // 2, 2), ALL_AXES)
    rows = P(ALL_AXES, None)
    placed = (
        rows,
        P(ALL_AXES, None, None),
        rows,
        rows,
        rows,
        rows,
        P(ALL_AXES, None, None),
        rows,
        P(None, ALL_AXES),
        P(),
        P(),
        P(),
    )
    return jax.shard_map(body, mesh=fine, in_specs=placed, out_specs=rows, check_vma=False)
```

profile of v0, /device:TPU:2, one launch (start us, length us, event | category | flops | bytes accessed | tf_op | source)
XLA Modules:
  0.0 380.8 jit_solution(17460445903867488199)
XLA Ops:
  7.3 1.6 broadcast_multiply_fusion.1
  9.0 40.9 %all_gather.13 = s32[32,32,2]{1,2,0:T(2,128)S(1)} all-gather(s32[1,32,2]{1,2,0:T(2,128)} %param.20), channel_id=1, replica_groups=mesh['x'=4,'y'=8,'z'=8,'core'=2] {'x','y'}, dimensions={0}, use_global_device_ids=true | all-gather | bytes 8448 | tf_op jit(solution)/shard_map/all_gather | solution.py:37
  50.8 1.5 gather_fusion
  52.3 33.0 %all-gather = s32[32,1,32]{2,1,0:T(1,128)S(1)} all-gather(s32[1,1,32]{2,1,0:T(1,128)} %bitcast.105), channel_id=1, replica_groups=mesh['x'=4,'y'=8,'z'=8,'core'=2] {'x','y'}, dimensions={0}, use_global_device_ids=true | all-gather | bytes 4224 | tf_op jit(solution)/shard_map/all_gather | solution.py:38
  85.3 0.7 dynamic-slice_reduce_fusion
  86.1 1.2 gather_fusion.1
  88.6 0.9 convolution_multiply_fusion
  89.5 9.0 %all-gather.4.cloned.1.call-done = bf16[96,128,128]{2,1,0:T(8,128)(2,1)} async-done(((bf16[3,128,128]{2,1,0:T(8,128)(2,1)}), bf16[96,128,128]{2,1,0:T(8,128)(2,1)}) %all-gather.4.cloned.1.call-update) | async-done | bytes 3145744 | tf_op jit(solution)/shard_map/all_gather | solution.py:58
  98.6 4.9 %gather_fusion.2 = bf16[128,128,128]{2,1,0:T(8,128)(2,1)} fusion(bf16[96,128,128]{2,1,0:T(8,128)(2,1)} %all-gather.4.cloned.1.call-done, s32[1024]{0:T(1024)S(1)} %pad_clamp_fusion.1), kind=kCustom, calls=%fused_computation.clone | custom fusion | bytes 8389120 | tf_op jit(solution)/shard_map/jit(_take)/gather | solution.py:59
  103.5 9.2 %fusion.13 = f32[128,128,128]{1,2,0:T(8,128)} fusion(bf16[128,128,128]{2,1,0:T(8,128)(2,1)} %param.15, bf16[128,128,128]{2,1,0:T(8,128)(2,1)} %gather_fusion.2, f32[128,128]{1,0:T(8,128)S(1)} %convolution_multiply_fusion, pred[128]{0:T(512)(128)(4,1)S(1)} %get-tuple-element.10), kind=kOutput, calls=%fused_computation.25 | convolution fusion | flops 545259520 | bytes 16842880 | tf_op jit(solution)/shard_map/tij,tjf->tif/dot_general | solution.py:61
  112.7 9.3 %copy.33 = f32[128,128,128]{0,2,1:T(8,128)} copy(f32[128,128,128]{1,2,0:T(8,128)} %fusion.13) | data formatting | bytes 16777216 | tf_op jit(solution)/shard_map/tij,tjf->tif/dot_general | solution.py:61
  122.1 4.0 %fusion.3 = (bf16[128,16384]{0,1:T(8,128)(2,1)S(1)}, bf16[128,16384]{0,1:T(8,128)(2,1)S(1)}) fusion(f32[128,128,128]{0,2,1:T(8,128)} %copy.33), kind=kLoop, calls=%fused_computation.13 | loop fusion | flops 8388608 | bytes 16777216 | tf_op jit(solution)/shard_map/convert_element_type | solution.py:66
  126.1 1.5 fusion.22
  127.7 1.5 fusion
  129.2 0.8 reshape.172
  130.0 1.3 copy.34
  131.4 15.8 %reduce-scatter.5.cloned.1.call-done = bf16[3072,128]{1,0:T(8,128)(2,1)} async-done(((bf16[6144,128]{1,0:T(8,128)(2,1)}), bf16[3072,128]{1,0:T(8,128)(2,1)}) %reduce-scatter.5.cloned.1.call-update) | async-done | bytes 786448 | tf_op jit(solution)/shard_map/reduce_scatter | solution.py:74
  147.7 45.3 %reduce-scatter.7.cloned.1.call-done = bf16[384,128]{1,0:T(8,128)(2,1)} async-done(((bf16[3072,128]{1,0:T(8,128)(2,1)}), bf16[384,128]{1,0:T(8,128)(2,1)}) %reduce-scatter.7.cloned.1.call-update) | async-done | bytes 98320 | tf_op jit(solution)/shard_map/reduce_scatter | solution.py:75
  193.1 1.1 fusion.34
  194.5 0.7 broadcast_multiply_fusion
  195.5 82.1 %all-gather.6.cloned.1.call-done = bf16[96,128,128]{2,1,0:T(8,128)(2,1)} async-done(((bf16[3,128,128]{2,1,0:T(8,128)(2,1)}), bf16[96,128,128]{2,1,0:T(8,128)(2,1)}) %all-gather.6.cloned.1.call-update) | async-done | bytes 3145744 | tf_op jit(solution)/shard_map/all_gather | solution.py:58
  277.6 4.9 %gather_fusion.3 = bf16[128,128,128]{2,1,0:T(8,128)(2,1)} fusion(bf16[96,128,128]{2,1,0:T(8,128)(2,1)} %all-gather.6.cloned.1.call-done, s32[1024]{0:T(1024)S(1)} %pad_clamp_fusion.1), kind=kCustom, calls=%fused_computation.1.clone | custom fusion | bytes 8389120 | tf_op jit(solution)/shard_map/jit(_take)/gather | solution.py:59
  282.5 9.2 %fusion.12 = f32[128,128,128]{1,2,0:T(8,128)} fusion(bf16[128,128,128]{2,1,0:T(8,128)(2,1)} %param.15, bf16[128,128,128]{2,1,0:T(8,128)(2,1)} %gather_fusion.3, f32[128,128]{1,0:T(8,128)S(1)} %convolution_multiply_fusion, pred[128]{0:T(512)(128)(4,1)S(1)} %get-tuple-element.10), kind=kOutput, calls=%fused_computation.24 | convolution fusion | flops 545259520 | bytes 16842880 | tf_op jit(solution)/shard_map/tij,tjf->tif/dot_general | solution.py:61
  291.8 9.3 %copy.38 = f32[128,128,128]{0,2,1:T(8,128)} copy(f32[128,128,128]{1,2,0:T(8,128)} %fusion.12) | data formatting | bytes 16777216 | tf_op jit(solution)/shard_map/tij,tjf->tif/dot_general | solution.py:61
  301.1 4.0 %fusion.2 = (bf16[128,16384]{0,1:T(8,128)(2,1)S(1)}, bf16[128,16384]{0,1:T(8,128)(2,1)S(1)}) fusion(f32[128,128,128]{0,2,1:T(8,128)} %copy.38), kind=kLoop, calls=%fused_computation.10 | loop fusion | flops 8388608 | bytes 16777216 | tf_op jit(solution)/shard_map/convert_element_type | solution.py:66
  305.1 1.5 fusion.21
  306.7 1.5 fusion.1
  308.2 0.8 reshape.177
  309.0 1.3 copy.39
  310.4 15.7 %reduce-scatter.9.cloned.1.call-done = bf16[3072,128]{1,0:T(8,128)(2,1)} async-done(((bf16[6144,128]{1,0:T(8,128)(2,1)}), bf16[3072,128]{1,0:T(8,128)(2,1)}) %reduce-scatter.9.cloned.1.call-update) | async-done | bytes 786448 | tf_op jit(solution)/shard_map/reduce_scatter | solution.py:74
  326.2 45.7 %reduce-scatter.11.cloned.1.call-done = bf16[384,128]{1,0:T(8,128)(2,1)} async-done(((bf16[3072,128]{1,0:T(8,128)(2,1)}), bf16[384,128]{1,0:T(8,128)(2,1)}) %reduce-scatter.11.cloned.1.call-update) | async-done | bytes 98320 | tf_op jit(solution)/shard_map/reduce_scatter | solution.py:75
  371.9 1.1 fusion.35
  (53 shorter events, 5.2 us)
Async XLA Ops:
  6.5 82.1 %copy-start = (bf16[535,128]{1,0:T(8,128)(2,1)S(1)}, bf16[535,128]{1,0:T(8,128)(2,1)}, u32[]{:S(2)}) copy-start(bf16[535,128]{1,0:T(8,128)(2,1)} %param.23) | copy-start | bytes 410884
  6.5 92.0 %all-gather.4.cloned.1.call-start = ((), (), s32[]{:S(2)}) async-start(), calls=%async_computation.4 | async-start | bytes 3244032 | tf_op jit(solution)/shard_map/all_gather | solution.py:58
  8.9 138.2 %reduce-scatter.5.cloned.1.call-start = ((), (), s32[]{:S(2)}) async-start(), calls=%async_computation.5 | async-start | bytes 2359296 | tf_op jit(solution)/shard_map/reduce_scatter | solution.py:74
  122.1 4.0 %copy-start.4 = (s32[1,128]{1,0:T(1,128)S(1)}, s32[1,128]{1,0:T(1,128)}, u32[]{:S(2)}) copy-start(s32[1,128]{1,0:T(1,128)} %param.19) | copy-start | bytes 1540
  129.2 18.0 %copy-start.3 = (bf16[2,64,64]{2,1,0:T(8,128)(2,1)S(1)}, bf16[2,64,64]{2,1,0:T(8,128)(2,1)}, u32[]{:S(2)}) copy-start(bf16[2,64,64]{2,1,0:T(8,128)(2,1)} %param.24) | copy-start | bytes 49156
  129.2 18.5 %copy-start.5 = (f32[2,64]{1,0:T(2,128)S(1)}, f32[2,64]{1,0:T(2,128)}, u32[]{:S(2)}) copy-start(f32[2,64]{1,0:T(2,128)} %param.25) | copy-start | bytes 1540
  130.0 64.4 %copy-start.2 = (bf16[384,128]{1,0:T(8,128)(2,1)S(1)}, bf16[384,128]{1,0:T(8,128)(2,1)}, u32[]{:S(2)}) copy-start(bf16[384,128]{1,0:T(8,128)(2,1)} %param.14) | copy-start | bytes 294916
  131.3 61.7 %reduce-scatter.7.cloned.1.call-start = ((), (), s32[]{:S(2)}) async-start(), calls=%async_computation.6 | async-start | bytes 884736 | tf_op jit(solution)/shard_map/reduce_scatter | solution.py:75
  147.2 130.5 %all-gather.6.cloned.1.call-start = ((), (), s32[]{:S(2)}) async-start(), calls=%async_computation.7 | async-start | bytes 3244032 | tf_op jit(solution)/shard_map/all_gather | solution.py:58
  195.2 130.9 %reduce-scatter.9.cloned.1.call-start = ((), (), s32[]{:S(2)}) async-start(), calls=%async_computation.8 | async-start | bytes 2359296 | tf_op jit(solution)/shard_map/reduce_scatter | solution.py:74
  308.2 65.7 %copy-start.1 = (bf16[535,128]{1,0:T(8,128)(2,1)S(1)}, bf16[535,128]{1,0:T(8,128)(2,1)}, u32[]{:S(2)}) copy-start(bf16[535,128]{1,0:T(8,128)(2,1)} %param.23) | copy-start | bytes 410884
  310.3 61.6 %reduce-scatter.11.cloned.1.call-start = ((), (), s32[]{:S(2)}) async-start(), calls=%async_computation.9 | async-start | bytes 884736 | tf_op jit(solution)/shard_map/reduce_scatter | solution.py:75
Sparse Core Ops, SparseCore 0:
  10.5 88.0 all-gather.3
  131.4 15.6 reduce-scatter.4
  150.0 43.0 reduce-scatter.6
  196.1 81.4 all-gather.5
  310.4 15.6 reduce-scatter.8
  328.8 43.0 reduce-scatter.10
where the time goes:
time: 381 us
  waiting for transfers between devices  214 us (56%)
  blocking collectives  74 us (19%)
  local copies, waits for them, and re-layouts  36.9 us (10%)
  matrix products  27.7 us (7%)
  other arithmetic  14.3 us (4%)
  between operations  13.8 us (4%)
    all_gather x2, waiting for transfers between devices, body(): gathered = lax.all_gather(blocks, NODE_AXES, axis=0, tiled=True)  91.2 us
    reduce_scatter x2, waiting for transfers between devices, body(): summed = lax.psum_scatter(half, 'z', scatter_dimension=0, tiled=True)  91 us
    all_gather x1, blocking collectives, body(): lists_all = lax.all_gather(send_blocks[0], NODE_AXES, axis=0, tiled=False)  40.9 us
    all_gather x1, blocking collectives, body(): counts_all = lax.all_gather(send_count[0], NODE_AXES, axis=0, tiled=False)  33 us
    reduce_scatter x2, waiting for transfers between devices, body(): half = lax.psum_scatter(by_core, 'core', scatter_dimension=0, tiled=True)  31.5 us
    dot_general x2, local copies, waits for them, and re-layouts, body(): jnp.einsum('tij,tjf->tif', adjacency, modulated, preferred_element_type=j...  18.6 us
    dot_general x2, matrix products, body(): jnp.einsum('tij,tjf->tif', adjacency, modulated, preferred_element_type=j...  18.5 us
    gather x2, local copies, waits for them, and re-layouts, body(): source_rows = jnp.take(gathered, source_index, axis=0)  9.87 us
  transfers between devices with their start and end apart: 6, of which 6 were waited for; matrix products, arithmetic and copies ran while one was open for 2% of the time, Pallas kernels for 0%

commit v1 on v0

--- a/solution.py
+++ b/solution.py
@@ -55,7 +55,9 @@
         blocks = states.reshape(own_blocks, size_block, width) * active[layer][
             :, None, None
         ].astype(jnp.bfloat16)
-        gathered = lax.all_gather(blocks, NODE_AXES, axis=0, tiled=True)
+        gathered = jnp.concatenate(
+            lax.all_to_all(jnp.stack([blocks] * lax.axis_size(NODE_AXES)), NODE_AXES, 0, 0), axis=0
+        )
         source_rows = jnp.take(gathered, source_index, axis=0)
         modulated = (source_rows * rel_rows[:, None, :]).astype(jnp.bfloat16)
         products = jnp.einsum(

time: 381 us -> 433 us (1.14)
  blocking collectives: 74 us -> 210 us
  waiting for transfers between devices: 214 us -> 124 us
  starting transfers between devices: 0.39 us -> 10.5 us
    all_gather x2 -> x0, waiting for transfers between devices: 91.2 us -> none  [body(): gathered = lax.all_gather(blocks, NODE_AXES, axis=0, tiled=True)]
    all_to_all x0 -> x1, blocking collectives: none -> 75.7 us  [body(): lax.all_to_all(jnp.stack([blocks] * lax.axis_size(NODE_AXES)), NODE_AXES,...]
    all_gather x1, blocking collectives: 40.9 us -> 102 us  [body(): lists_all = lax.all_gather(send_blocks[0], NODE_AXES, axis=0, tiled=False)]
    all_to_all x0 -> x1, starting transfers between devices: none -> 10.4 us  [body(): lax.all_to_all(jnp.stack([blocks] * lax.axis_size(NODE_AXES)), NODE_AXES,...]
  transfers between devices with their start and end apart: 6 -> 5, of which waited for: 6 -> 4; matrix products, arithmetic and copies ran while one was open for 2% -> 1% of each run, Pallas kernels for 0% -> 0%
where the time goes in v1:
time: 433 us
  blocking collectives  210 us (48%)
  waiting for transfers between devices  124 us (29%)
  local copies, waits for them, and re-layouts  36.5 us (8%)
  matrix products  27.1 us (6%)
  between operations  13.5 us (3%)
  other arithmetic  11 us (3%)
  starting transfers between devices  10.5 us (2%)
    all_gather x1, blocking collectives, body(): lists_all = lax.all_gather(send_blocks[0], NODE_AXES, axis=0, tiled=False)  102 us
    reduce_scatter x2, waiting for transfers between devices, body(): summed = lax.psum_scatter(half, 'z', scatter_dimension=0, tiled=True)  91 us
    all_to_all x1, blocking collectives, body(): lax.all_to_all(jnp.stack([blocks] * lax.axis_size(NODE_AXES)), NODE_AXES,...  75.7 us
    reduce_scatter x2, waiting for transfers between devices, body(): half = lax.psum_scatter(by_core, 'core', scatter_dimension=0, tiled=True)  32.9 us
    all_gather x1, blocking collectives, body(): counts_all = lax.all_gather(send_count[0], NODE_AXES, axis=0, tiled=False)  32.5 us
    dot_general x2, local copies, waits for them, and re-layouts, body(): jnp.einsum('tij,tjf->tif', adjacency, modulated, preferred_element_type=j...  18.8 us
    dot_general x2, matrix products, body(): jnp.einsum('tij,tjf->tif', adjacency, modulated, preferred_element_type=j...  18.4 us
    all_to_all x1, starting transfers between devices, body(): lax.all_to_all(jnp.stack([blocks] * lax.axis_size(NODE_AXES)), NODE_AXES,...  10.4 us
  transfers between devices with their start and end apart: 5, of which 4 were waited for; matrix products, arithmetic and copies ran while one was open for 1% of the time, Pallas kernels for 0%

profile of v1, /device:TPU:2, one launch (start us, length us, event | category | flops | bytes accessed | tf_op | source)
XLA Modules:
  0.0 432.8 jit_solution(3218005651048108618)
XLA Ops:
  7.3 1.0 broadcast_multiply_fusion.1
  8.3 2.4 stack.4
  10.7 10.4 %all-to-all-start = ((bf16[32,3,128,128]{3,2,1,0:T(8,128)(2,1)}), bf16[32,3,128,128]{3,2,1,0:T(8,128)(2,1)S(1)}, u32[]{:S(2)}, u32[]{:S(2)}) async-start(bf16[32,3,128,128]{3,2,1,0:T(8,128)(2,1)} %stack.4), calls=%async_computation | async-start | bytes 6291456 | tf_op jit(solution)/shard_map/all_to_all | solution.py:59
  21.1 101.9 %all_gather.6 = s32[32,32,2]{1,2,0:T(2,128)S(1)} all-gather(s32[1,32,2]{1,2,0:T(2,128)S(1)} %copy-done.6), channel_id=1, replica_groups=mesh['x'=4,'y'=8,'z'=8,'core'=2] {'x','y'}, dimensions={0}, use_global_device_ids=true | all-gather | bytes 8448 | tf_op jit(solution)/shard_map/all_gather | solution.py:37
  123.3 1.5 gather_fusion
  124.8 32.5 %all-gather = s32[32,1,32]{2,1,0:T(1,128)S(1)} all-gather(s32[1,1,32]{2,1,0:T(1,128)S(1)} %bitcast.109), channel_id=1, replica_groups=mesh['x'=4,'y'=8,'z'=8,'core'=2] {'x','y'}, dimensions={0}, use_global_device_ids=true | all-gather | bytes 4224 | tf_op jit(solution)/shard_map/all_gather | solution.py:38
  157.3 0.7 dynamic-slice_reduce_fusion
  158.1 1.2 gather_fusion.1
  159.6 3.0 gather_fusion.2
  162.7 9.2 %fusion.13 = f32[128,128,128]{1,2,0:T(8,128)} fusion(bf16[128,128,128]{2,1,0:T(8,128)(2,1)} %param.15, bf16[128,128,128]{2,1,0:T(8,128)(2,1)} %gather_fusion.2, f32[128,128]{1,0:T(8,128)S(1)} %convolution_multiply_fusion, pred[128]{0:T(512)(128)(4,1)S(1)} %get-tuple-element.10), kind=kOutput, calls=%fused_computation.25 | convolution fusion | flops 545259520 | bytes 16842880 | tf_op jit(solution)/shard_map/tij,tjf->tif/dot_general | solution.py:63
  171.9 9.4 %copy.33 = f32[128,128,128]{0,2,1:T(8,128)} copy(f32[128,128,128]{1,2,0:T(8,128)} %fusion.13) | data formatting | bytes 16777216 | tf_op jit(solution)/shard_map/tij,tjf->tif/dot_general | solution.py:63
  181.3 4.0 fusion.3
  185.4 1.5 fusion.22
  186.9 1.5 fusion
  188.5 0.8 reshape.185
  189.3 1.3 copy.34
  190.6 19.4 %reduce-scatter.5.cloned.1.call-done = bf16[3072,128]{1,0:T(8,128)(2,1)} async-done(((bf16[6144,128]{1,0:T(8,128)(2,1)}), bf16[3072,128]{1,0:T(8,128)(2,1)}) %reduce-scatter.5.cloned.1.call-update) | async-done | bytes 786448 | tf_op jit(solution)/shard_map/reduce_scatter | solution.py:76
  210.7 45.3 %reduce-scatter.7.cloned.1.call-done = bf16[384,128]{1,0:T(8,128)(2,1)} async-done(((bf16[3072,128]{1,0:T(8,128)(2,1)}), bf16[384,128]{1,0:T(8,128)(2,1)}) %reduce-scatter.7.cloned.1.call-update) | async-done | bytes 98320 | tf_op jit(solution)/shard_map/reduce_scatter | solution.py:77
  256.0 1.1 fusion.34
  257.5 0.8 stack.5
  258.3 75.7 %all_to_all.10 = bf16[32,3,128,128]{3,2,1,0:T(8,128)(2,1)S(1)} all-to-all(bf16[32,3,128,128]{3,2,1,0:T(8,128)(2,1)S(1)} %stack.5), channel_id=1, replica_groups=mesh['x'=4,'y'=8,'z'=8,'core'=2] {'x','y'}, dimensions={0} | all-to-all | bytes 6291456 | tf_op jit(solution)/shard_map/all_to_all | solution.py:59
  334.0 3.0 gather_fusion.3
  337.0 9.2 %fusion.12 = f32[128,128,128]{1,2,0:T(8,128)} fusion(bf16[128,128,128]{2,1,0:T(8,128)(2,1)} %param.15, bf16[128,128,128]{2,1,0:T(8,128)(2,1)} %gather_fusion.3, f32[128,128]{1,0:T(8,128)S(1)} %convolution_multiply_fusion, pred[128]{0:T(512)(128)(4,1)S(1)} %get-tuple-element.10), kind=kOutput, calls=%fused_computation.24 | convolution fusion | flops 545259520 | bytes 16842880 | tf_op jit(solution)/shard_map/tij,tjf->tif/dot_general | solution.py:63
  346.3 9.4 %copy.38 = f32[128,128,128]{0,2,1:T(8,128)} copy(f32[128,128,128]{1,2,0:T(8,128)} %fusion.12) | data formatting | bytes 16777216 | tf_op jit(solution)/shard_map/tij,tjf->tif/dot_general | solution.py:63
  355.7 4.0 fusion.2
  359.7 1.5 fusion.21
  361.2 1.5 fusion.1
  362.8 0.8 reshape.191
  363.6 1.3 copy.39
  364.9 13.5 %reduce-scatter.9.cloned.1.call-done = bf16[3072,128]{1,0:T(8,128)(2,1)} async-done(((bf16[6144,128]{1,0:T(8,128)(2,1)}), bf16[3072,128]{1,0:T(8,128)(2,1)}) %reduce-scatter.9.cloned.1.call-update) | async-done | bytes 786448 | tf_op jit(solution)/shard_map/reduce_scatter | solution.py:76
  378.5 45.6 %reduce-scatter.11.cloned.1.call-done = bf16[384,128]{1,0:T(8,128)(2,1)} async-done(((bf16[3072,128]{1,0:T(8,128)(2,1)}), bf16[384,128]{1,0:T(8,128)(2,1)}) %reduce-scatter.11.cloned.1.call-update) | async-done | bytes 98320 | tf_op jit(solution)/shard_map/reduce_scatter | solution.py:77
  424.2 1.1 fusion.35
  (62 shorter events, 3.4 us)
Async XLA Ops:
  6.5 152.8 %copy-start = (bf16[535,128]{1,0:T(8,128)(2,1)S(1)}, bf16[535,128]{1,0:T(8,128)(2,1)}, u32[]{:S(2)}) copy-start(bf16[535,128]{1,0:T(8,128)(2,1)} %param.23) | copy-start | bytes 410884
  8.2 12.9 %copy-start.6 = (s32[1,32,2]{1,2,0:T(2,128)S(1)}, s32[1,32,2]{1,2,0:T(2,128)}, u32[]{:S(2)}) copy-start(s32[1,32,2]{1,2,0:T(2,128)} %param.20) | copy-start | bytes 772
  8.2 115.0 %copy-start.5 = (s32[1,128]{1,0:T(1,128)S(1)}, s32[1,128]{1,0:T(1,128)}, u32[]{:S(2)}) copy-start(s32[1,128]{1,0:T(1,128)} %param.16) | copy-start | bytes 1540
  8.3 115.0 %copy-start.9 = (s32[1,128]{1,0:T(1,128)S(1)}, s32[1,128]{1,0:T(1,128)}, u32[]{:S(2)}) copy-start(s32[1,128]{1,0:T(1,128)} %param.17) | copy-start | bytes 1540
  10.7 114.1 %copy-start.8 = (s32[1,32]{1,0:T(1,128)S(1)}, s32[1,32]{1,0:T(1,128)}, u32[]{:S(2)}) copy-start(s32[1,32]{1,0:T(1,128)} %param.21) | copy-start | bytes 388
  10.7 148.7 %copy-start.10 = (s32[1,128]{1,0:T(1,128)S(1)}, s32[1,128]{1,0:T(1,128)}, u32[]{:S(2)}) copy-start(s32[1,128]{1,0:T(1,128)} %param.18) | copy-start | bytes 1540
  10.7 148.9 %all-to-all-start = ((bf16[32,3,128,128]{3,2,1,0:T(8,128)(2,1)}), bf16[32,3,128,128]{3,2,1,0:T(8,128)(2,1)S(1)}, u32[]{:S(2)}, u32[]{:S(2)}) async-start(bf16[32,3,128,128]{3,2,1,0:T(8,128)(2,1)} %stack.4), calls=%async_computation | async-start | bytes 6291456 | tf_op jit(solution)/shard_map/all_to_all | solution.py:59
  21.1 189.0 %reduce-scatter.5.cloned.1.call-start = ((), (), s32[]{:S(2)}) async-start(), calls=%async_computation.6 | async-start | bytes 2359296 | tf_op jit(solution)/shard_map/reduce_scatter | solution.py:76
  181.3 4.0 copy-start.4
  188.5 21.7 %copy-start.3 = (bf16[2,64,64]{2,1,0:T(8,128)(2,1)S(1)}, bf16[2,64,64]{2,1,0:T(8,128)(2,1)}, u32[]{:S(2)}) copy-start(bf16[2,64,64]{2,1,0:T(8,128)(2,1)} %param.24) | copy-start | bytes 49156
  188.5 22.2 %copy-start.7 = (f32[2,64]{1,0:T(2,128)S(1)}, f32[2,64]{1,0:T(2,128)}, u32[]{:S(2)}) copy-start(f32[2,64]{1,0:T(2,128)} %param.25) | copy-start | bytes 1540
  189.3 68.1 %copy-start.2 = (bf16[384,128]{1,0:T(8,128)(2,1)S(1)}, bf16[384,128]{1,0:T(8,128)(2,1)}, u32[]{:S(2)}) copy-start(bf16[384,128]{1,0:T(8,128)(2,1)} %param.14) | copy-start | bytes 294916
  190.6 65.4 %reduce-scatter.7.cloned.1.call-start = ((), (), s32[]{:S(2)}) async-start(), calls=%async_computation.7 | async-start | bytes 884736 | tf_op jit(solution)/shard_map/reduce_scatter | solution.py:77
  210.1 168.3 %reduce-scatter.9.cloned.1.call-start = ((), (), s32[]{:S(2)}) async-start(), calls=%async_computation.8 | async-start | bytes 2359296 | tf_op jit(solution)/shard_map/reduce_scatter | solution.py:76
  362.8 63.4 %copy-start.1 = (bf16[535,128]{1,0:T(8,128)(2,1)S(1)}, bf16[535,128]{1,0:T(8,128)(2,1)}, u32[]{:S(2)}) copy-start(bf16[535,128]{1,0:T(8,128)(2,1)} %param.23) | copy-start | bytes 410884
  364.9 59.3 %reduce-scatter.11.cloned.1.call-start = ((), (), s32[]{:S(2)}) async-start(), calls=%async_computation.9 | async-start | bytes 884736 | tf_op jit(solution)/shard_map/reduce_scatter | solution.py:77
Sparse Core Ops, SparseCore 0:
  190.7 19.3 reduce-scatter.4
  212.9 43.0 reduce-scatter.6
  365.0 13.3 reduce-scatter.8
  381.1 43.0 reduce-scatter.10
